TPU v7x, 32 devices: a whole 2x2x4 slice. The times are simulated.
32 devices in a mesh: grid: 4 (over z), mode: 8 (over y, x, core).
Axes of the slice: x: 2, y: 2, z: 4, core: 2. Of those that a mesh axis runs over, the one named last changes fastest.
Arguments:
- modes_field: bfloat16 [512, 192, 1024], P('mode', 'grid'), may hold values from -6 to 6
- chaos_basis: bfloat16 [512, 512], replicated, may hold values from -0.25 to 0.25
- node_weights: float32 [512], replicated, may hold values from 0.5 to 2
- node_points: float32 [512, 16], replicated, may hold values from -4 to 4
- kl_fields: float32 [16, 192, 1024], P(None, 'grid'), may hold values from -0.6 to 0.6
- velocity: float32 [2, 192, 1024], P(None, 'grid'), may hold values from -4 to 4
Outputs:
- tendency: bfloat16 [512, 192, 1024], P('mode', 'grid')
All inputs are finite; a program needn't handle non-finite values.
Results may differ from a plain program's by a relative error of at most 0.0053.
Values may be sent and summed in bfloat16 or wider, within the bound.
No kernel may reach another device: no remote copies, remote signals or barrier semaphores. Data moves between devices by JAX's collectives and lax.ppermute only.
A program may use at most 128 MiB of HBM per device.

v0:
```python
import jax
import jax.numpy as jnp
from jax import lax
from jax.sharding import PartitionSpec as P


def extended(cells, sides, width):
    for axis, dim in sides:
        count = lax.axis_size(axis)
        ends = count - 1
        head = lax.slice_in_dim(cells, 0, width, axis=dim)
        tail = lax.slice_in_dim(cells, cells.shape[dim] - width, cells.shape[dim], axis=dim)
        cells = jnp.concatenate(
            [
                lax.ppermute(tail, axis, [(i, (i + 1) % count) for i in range(ends)]),
                cells,
                lax.ppermute(head, axis, [((i + 1) % count, i) for i in range(ends)]),
            ],
            axis=dim,
        )
    return cells


def node_terms(padded_field, kl_piece, node_points, velocity_piece, node_weights):
    field_value = padded_field.astype(jnp.float32)
    viscosity = jnp.exp(
        jnp.einsum("qk,krc->qrc", node_points, kl_piece, precision=lax.Precision.HIGHEST)
    )
    center = field_value[:, 1:-1, 1:-1]
    visc_center = viscosity[:, 1:-1, 1:-1]

    def face_flux(near_field, near_visc):
        return 0.5 * (visc_center + near_visc) * (near_field - center)

    north = field_value[:, 2:, 1:-1]
    south = field_value[:, :-2, 1:-1]
    east = field_value[:, 1:-1, 2:]
    west = field_value[:, 1:-1, :-2]
    diffusion = face_flux(north, viscosity[:, 2:, 1:-1]) + face_flux(south, viscosity[:, :-2, 1:-1])
    diffusion = (
        diffusion
        + face_flux(east, viscosity[:, 1:-1, 2:])
        + face_flux(west, viscosity[:, 1:-1, :-2])
    )
    advection = 0.5 * velocity_piece[0] * (north - south) + 0.5 * velocity_piece[1] * (east - west)
    flux = diffusion - advection
    return (node_weights[:, None, None] * flux).astype(jnp.bfloat16)


def local(modes_field, chaos_basis, node_weights, node_points, kl_fields, velocity):
    kl_rimmed = extended(kl_fields, (("grid", 1),), 1)
    kl_rimmed = jnp.pad(kl_rimmed, ((0, 0), (0, 0), (1, 1)))
    result = jnp.einsum(
        "qp,prc->qrc",
        chaos_basis,
        lax.all_to_all(modes_field, "mode", split_axis=2, concat_axis=0, tiled=True),
        preferred_element_type=jnp.float32,
    )
    nodal = result.astype(jnp.bfloat16)
    node_blocks = lax.all_to_all(nodal, "mode", split_axis=0, concat_axis=2, tiled=True)
    rimmed = extended(node_blocks, (("grid", 1),), 1)
    padded_field = jnp.pad(rimmed, ((0, 0), (0, 0), (1, 1)))
    node_share = node_blocks.shape[0]
    first_index = lax.axis_index("mode") * node_share
    point_part = lax.dynamic_slice_in_dim(node_points, first_index, node_share, 0)
    weight_part = lax.dynamic_slice_in_dim(node_weights, first_index, node_share, 0)
    weighted = node_terms(padded_field, kl_rimmed, point_part, velocity, weight_part)
    cell_terms = lax.all_to_all(weighted, "mode", split_axis=2, concat_axis=0, tiled=True)
    tendency = jnp.einsum(
        "qp,qrc->prc", chaos_basis, cell_terms, preferred_element_type=jnp.float32
    )
    tendency = tendency.astype(jnp.bfloat16)
    return lax.all_to_all(tendency, "mode", split_axis=0, concat_axis=2, tiled=True)


def solution(mesh):
    return jax.shard_map(
        local,
        mesh=mesh,
        in_specs=(
            P("mode", "grid", None),
            P(),
            P(),
            P(),
            P(None, "grid", None),
            P(None, "grid", None),
        ),
        out_specs=P("mode", "grid", None),
        check_vma=False,
    )
```

profile of v0, /device:TPU:0, one launch (start us, length us, event | category | flops | bytes accessed | tf_op | source)
XLA Modules:
  0.0 571.1 jit_solution(2297330801579381977)
XLA Ops:
  0.0 0.0 copy-start
  0.0 20.8 %copy.58 = bf16[64,48,1024]{0,1,2:T(8,128)(2,1)} copy(bf16[64,48,1024]{2,1,0:T(8,128)(2,1)} %param.6) | data formatting | bytes 12582912 | tf_op args[0]
  20.8 13.7 %reshape.3 = bf16[8,2,196608]{2,1,0:T(2,128)(2,1)} reshape(bf16[1024,48,64]{2,1,0:T(8,128)(2,1)} %bitcast.48) | data formatting | bytes 12582912
  34.5 77.6 %all_to_all.72 = bf16[8,2,196608]{2,1,0:T(2,128)(2,1)} all-to-all(bf16[8,2,196608]{2,1,0:T(2,128)(2,1)} %reshape.3), channel_id=1, replica_groups=mesh['grid'=4,'mode'=8] {'mode'}, dimensions={0} | all-to-all | bytes 12582912 | tf_op jit(solution)/shard_map/all_to_all | solution.py:56
  112.1 13.3 %reshape.4 = bf16[1024,48,64]{2,1,0:T(8,128)(2,1)} reshape(bf16[8,2,196608]{2,1,0:T(2,128)(2,1)} %all_to_all.72) | data formatting | bytes 12582912
  125.4 14.1 %copy.59 = bf16[64,48,8,128]{3,0,2,1:T(8,128)(2,1)} copy(bf16[64,48,8,128]{0,1,3,2:T(8,128)(2,1)} %bitcast.45) | data formatting | bytes 12582912 | tf_op jit(solution)/shard_map/all_to_all | solution.py:56
  139.5 0.0 copy-done
  139.5 6.4 %convolution_convert_fusion = bf16[512,48,128]{2,0,1:T(8,128)(2,1)S(1)} fusion(bf16[512,48,128]{2,0,1:T(8,128)(2,1)} %bitcast.54, bf16[512,512]{1,0:T(8,128)(2,1)S(1)} %copy-done), kind=kOutput, calls=%fused_computation.40 | convolution fusion | flops 3224371200 | bytes 13107200 | tf_op jit(solution)/shard_map/qp,prc->qrc/dot_general | solution.py:53
  145.9 6.8 %copy.60 = bf16[512,48,128]{2,1,0:T(8,128)(2,1)} copy(bf16[512,48,128]{2,0,1:T(8,128)(2,1)S(1)} %convolution_convert_fusion) | data formatting | bytes 12582912 | tf_op jit(solution)/shard_map/convert_element_type | solution.py:59
  152.7 0.0 copy-start.2
  152.7 5.1 all-to-all-start.1
  157.8 3.7 copy.55
  161.5 0.0 copy-start.1
  161.5 1.7 copy-done.1
  163.2 4.3 collective-permute-start
  167.5 1.3 collective-permute-start.1
  168.8 0.8 dynamic_slice.6
  169.5 0.0 copy-done.2
  169.6 59.6 %all-to-all-done.1 = bf16[512,48,128]{2,1,0:T(8,128)(2,1)} async-done(((bf16[512,48,128]{2,1,0:T(8,128)(2,1)}), bf16[512,48,128]{2,1,0:T(8,128)(2,1)}, u32[]{:S(2)}, u32[]{:S(2)}) %all-to-all-start.1) | async-done | bytes 6291488 | tf_op jit(solution)/shard_map/all_to_all | solution.py:60
  229.2 9.5 %copy.75 = bf16[8,64,48,128]{3,0,1,2:T(8,128)(2,1)} copy(bf16[8,64,48,128]{3,2,1,0:T(8,128)(2,1)} %bitcast.5) | data formatting | bytes 12582912 | tf_op jit(solution)/shard_map/all_to_all | solution.py:60
  238.7 10.3 %all_to_all.59 = bf16[64,48,1024]{2,0,1:T(8,128)(2,1)} reshape(bf16[64,48,8,128]{3,2,0,1:T(8,128)(2,1)} %bitcast.51) | data formatting | bytes 12582912 | tf_op jit(solution)/shard_map/all_to_all | solution.py:60
  249.0 0.0 slice-start
  249.0 1.1 fusion.39
  250.2 4.4 collective-permute-start.2
  254.6 0.0 slice-start.1
  254.6 1.6 collective-permute-start.3
  256.2 0.0 collective-permute-done
  256.2 0.0 collective-permute-done.1
  256.2 16.3 %convolution_exponential_fusion = f32[64,50,1026]{2,0,1:T(8,128)} fusion(f32[16,1,1024]{2,0,1:T(8,128)S(1)} %collective-permute-done.1, f32[16,48,1024]{2,0,1:T(8,128)} %copy-done.1, f32[16,1,1024]{2,0,1:T(8,128)S(1)} %collective-permute-done, f32[512,16]{0,1:T(8,128)} %param.9, s32[]{:T(128)S(6)} %select_n.4), kind=kOutput, calls=%fused_computation.2 | convolution fusion | flops 636940800 | bytes 16417796 | tf_op jit(solution)/shard_map/qk,krc->qrc/dot_general | solution.py:27
  272.5 0.0 collective-permute-done.2
  272.5 0.0 collective-permute-done.3
  272.5 0.0 slice-done
  272.5 0.0 slice-done.1
  272.5 7.0 %fusion.20 = f32[64,50,1026]{2,0,1:T(8,128)} fusion(bf16[64,1,1024]{2,0,1:T(8,128)(2,1)S(1)} %collective-permute-done.3, bf16[64,48,1024]{2,0,1:T(8,128)(2,1)S(1)} %bitcast.50, bf16[64,1,1024]{2,0,1:T(8,128)(2,1)S(1)} %collective-permute-done.2), kind=kLoop, calls=%fused_computation.27 | loop fusion | flops 39398400 | bytes 19686400 | tf_op jit(solution)/shard_map/convert_element_type | solution.py:25
  279.5 60.8 %fusion.6 = bf16[64,48,1024]{2,0,1:T(8,128)(2,1)} fusion(f32[64,50,1026]{2,0,1:T(8,128)} %convolution_exponential_fusion, f32[64,50,1026]{2,0,1:T(8,128)} %fusion.20, f32[48,1024]{1,0:T(8,128)S(1)} %get-tuple-element.10, f32[48,1024]{1,0:T(8,128)S(1)} %get-tuple-element.9, f32[64]{0:T(128)S(1)} %dynamic_slice.6), kind=kLoop, calls=%fused_computation.10 | loop fusion | flops 84934656 | bytes 132514048 | tf_op jit(solution)/shard_map/convert_element_type | solution.py:47
  340.4 15.7 %copy.62 = bf16[64,48,1024]{0,1,2:T(8,128)(2,1)} copy(bf16[64,48,1024]{2,0,1:T(8,128)(2,1)} %fusion.6) | data formatting | bytes 12582912 | tf_op jit(solution)/shard_map/convert_element_type | solution.py:47
  356.1 13.7 %reshape.5 = bf16[8,2,196608]{2,1,0:T(2,128)(2,1)} reshape(bf16[1024,48,64]{2,1,0:T(8,128)(2,1)} %bitcast.46) | data formatting | bytes 12582912
  369.8 76.9 %all_to_all.73 = bf16[8,2,196608]{2,1,0:T(2,128)(2,1)} all-to-all(bf16[8,2,196608]{2,1,0:T(2,128)(2,1)} %reshape.5), channel_id=1, replica_groups=mesh['grid'=4,'mode'=8] {'mode'}, dimensions={0} | all-to-all | bytes 12582912 | tf_op jit(solution)/shard_map/all_to_all | solution.py:68
  446.7 13.3 %reshape.6 = bf16[1024,48,64]{2,1,0:T(8,128)(2,1)} reshape(bf16[8,2,196608]{2,1,0:T(2,128)(2,1)} %all_to_all.73) | data formatting | bytes 12582912
  460.0 14.1 %copy.70 = bf16[8,64,48,128]{3,1,0,2:T(8,128)(2,1)} copy(bf16[8,64,48,128]{1,2,3,0:T(8,128)(2,1)} %bitcast.47) | data formatting | bytes 12582912 | tf_op jit(solution)/shard_map/all_to_all | solution.py:68
  474.1 8.2 %convert_bitcast_fusion = bf16[512,48,128]{0,2,1:T(8,128)(2,1)} fusion(bf16[512,48,128]{2,0,1:T(8,128)(2,1)} %bitcast.53, bf16[512,512]{1,0:T(8,128)(2,1)S(1)} %copy-done), kind=kOutput, calls=%fused_computation.30 | convolution fusion | flops 3224371200 | bytes 13107200 | tf_op jit(solution)/shard_map/qp,qrc->prc/dot_general | solution.py:69
  482.4 9.0 %copy.66 = bf16[512,48,128]{2,1,0:T(8,128)(2,1)} copy(bf16[512,48,128]{0,2,1:T(8,128)(2,1)} %convert_bitcast_fusion) | data formatting | bytes 12582912 | tf_op jit(solution)/shard_map/convert_element_type | solution.py:72
  491.3 75.2 %all_to_all.74 = bf16[512,48,128]{2,1,0:T(8,128)(2,1)S(1)} all-to-all(bf16[512,48,128]{2,1,0:T(8,128)(2,1)} %copy.66), channel_id=1, replica_groups=mesh['grid'=4,'mode'=8] {'mode'}, dimensions={0} | all-to-all | bytes 12582912 | tf_op jit(solution)/shard_map/all_to_all | solution.py:73
  566.5 4.5 copy.74
  (3 shorter events, 0.0 us)
Async XLA Ops:
  0.0 139.5 %copy-start = (bf16[512,512]{1,0:T(8,128)(2,1)S(1)}, bf16[512,512]{1,0:T(8,128)(2,1)}, u32[]{:S(2)}) copy-start(bf16[512,512]{1,0:T(8,128)(2,1)} %param.7) | copy-start | bytes 1572868
  152.7 16.8 %copy-start.2 = (f32[2,48,1024]{2,1,0:T(8,128)S(1)}, f32[2,48,1024]{2,1,0:T(8,128)}, u32[]{:S(2)}) copy-start(f32[2,48,1024]{2,1,0:T(8,128)} %param.11) | copy-start | bytes 1179652
  152.7 76.5 %all-to-all-start.1 = ((bf16[512,48,128]{2,1,0:T(8,128)(2,1)}), bf16[512,48,128]{2,1,0:T(8,128)(2,1)}, u32[]{:S(2)}, u32[]{:S(2)}) async-start(bf16[512,48,128]{2,1,0:T(8,128)(2,1)} %copy.60), calls=%async_computation.1 | async-start | bytes 12582912 | tf_op jit(solution)/shard_map/all_to_all | solution.py:60
  161.5 1.7 copy-start.1
  163.2 93.0 %collective-permute-start = (f32[16,1,1024]{2,0,1:T(8,128)S(1)}, f32[16,1,1024]{2,0,1:T(8,128)S(1)}, u32[]{:S(2)}, u32[]{:S(2)}) collective-permute-start(f32[16,1,1024]{2,0,1:T(8,128)S(1)} %get-tuple-element.7), channel_id=1, source_target_pairs={{0,8},{8,16},{16,24},{1,9},{9,17},{17,25},{2,10},{10,18},{18,26},{... | collective-permute-start | bytes 196616 | tf_op jit(solution)/shard_map/ppermute | solution.py:15
  167.5 88.8 %collective-permute-start.1 = (f32[16,1,1024]{2,0,1:T(8,128)S(1)}, f32[16,1,1024]{2,0,1:T(8,128)S(1)}, u32[]{:S(2)}, u32[]{:S(2)}) collective-permute-start(f32[16,1,1024]{2,0,1:T(8,128)S(1)} %get-tuple-element.8), channel_id=1, source_target_pairs={{8,0},{16,8},{24,16},{9,1},{17,9},{25,17},{10,2},{18,10},{26,18},{... | collective-permute-start | bytes 196616 | tf_op jit(solution)/shard_map/ppermute | solution.py:17
  249.0 23.5 %slice-start = ((s8[6291456]{0:T(1024)(128)(4,1)}), s8[4194304]{0:T(1024)(128)(4,1)S(1)}, s32[]{:S(2)}) async-start(s8[6291456]{0:T(1024)(128)(4,1)} %bitcast.49), calls=%async_computation.4 | async-start | bytes 8388608
  250.2 22.3 %collective-permute-start.2 = (bf16[64,1,1024]{2,0,1:T(8,128)(2,1)S(1)}, bf16[64,1,1024]{2,0,1:T(8,128)(2,1)S(1)}, u32[]{:S(2)}, u32[]{:S(2)}) collective-permute-start(bf16[64,1,1024]{2,0,1:T(8,128)(2,1)S(1)} %get-tuple-element.5), channel_id=1, source_target_pairs={{0,8},{8,16},{16,24},{1,9},{9,17},{17,25},{2,10},{10,18},{18,26},{... | collective-permute-start | bytes 393224 | tf_op jit(solution)/shard_map/ppermute | solution.py:15
  254.6 18.0 %slice-start.1 = ((s8[6291456]{0:T(1024)(128)(4,1)}), s8[2097152]{0:T(1024)(128)(4,1)S(1)}, s32[]{:S(2)}) async-start(s8[6291456]{0:T(1024)(128)(4,1)} %bitcast.49), calls=%async_computation.5 | async-start | bytes 4194304
  254.6 17.9 %collective-permute-start.3 = (bf16[64,1,1024]{2,0,1:T(8,128)(2,1)S(1)}, bf16[64,1,1024]{2,0,1:T(8,128)(2,1)S(1)}, u32[]{:S(2)}, u32[]{:S(2)}) collective-permute-start(bf16[64,1,1024]{2,0,1:T(8,128)(2,1)S(1)} %get-tuple-element.6), channel_id=1, source_target_pairs={{8,0},{16,8},{24,16},{9,1},{17,9},{25,17},{10,2},{18,10},{26,18},{... | collective-permute-start | bytes 393224 | tf_op jit(solution)/shard_map/ppermute | solution.py:17
where the time goes:
time: 574 us; the launch traced here: 571 us
  blocking collectives  230 us (40%)
  local copies, waits for them, and re-layouts  166 us (29%)
  other arithmetic  67.9 us (12%)
  waiting for transfers between devices  59.6 us (10%)
  matrix products  30.9 us (5%)
  starting transfers between devices  16.7 us (3%)
    unnamed x16, local copies, waits for them, and re-layouts  80.3 us
    all_to_all x1, blocking collectives, local(): lax.all_to_all(modes_field, 'mode', split_axis=2, concat_axis=0, tiled=True)  77.6 us
    all_to_all x1, blocking collectives, local(): lax.all_to_all(weighted, 'mode', split_axis=2, concat_axis=0, tiled=True)  76.9 us
    all_to_all x1, blocking collectives, local(): lax.all_to_all(tendency, 'mode', split_axis=0, concat_axis=2, tiled=True)  75.2 us
    convert_element_type x1, other arithmetic, node_terms(): return (node_weights[:, None, None] * flux).astype(jnp.bfloat16)  60.8 us
    all_to_all x1, waiting for transfers between devices, local(): lax.all_to_all(nodal, 'mode', split_axis=0, concat_axis=2, tiled=True)  59.6 us
    all_to_all x2, local copies, waits for them, and re-layouts, local(): lax.all_to_all(nodal, 'mode', split_axis=0, concat_axis=2, tiled=True)  19.8 us
    dot_general x1, matrix products, node_terms(): jnp.einsum('qk,krc->qrc', node_points, kl_piece, precision=lax.Precision....  16.3 us
  transfers between devices with their start and end apart: 5, of which 1 were waited for; matrix products, arithmetic and copies ran while one was open for 6% of the time, Pallas kernels for 0%

commit v1 on v0

--- a/solution.py
+++ b/solution.py
@@ -53,7 +53,12 @@
     result = jnp.einsum(
         "qp,prc->qrc",
         chaos_basis,
-        lax.all_to_all(modes_field, "mode", split_axis=2, concat_axis=0, tiled=True),
+        jnp.concatenate(
+            lax.all_to_all(
+                jnp.stack(jnp.split(modes_field, lax.axis_size("mode"), axis=2)), "mode", 0, 0
+            ),
+            axis=0,
+        ),
         preferred_element_type=jnp.float32,
     )
     nodal = result.astype(jnp.bfloat16)

time: 574 us -> 522 us (0.909)
  local copies, waits for them, and re-layouts: 166 us -> 116 us
    unnamed x16 -> x20, local copies, waits for them, and re-layouts: 80.3 us -> 41.2 us
    all_to_all x1 -> x0, local copies, waits for them, and re-layouts: 14.1 us -> none  [local(): lax.all_to_all(modes_field, 'mode', split_axis=2, concat_axis=0, tiled=True)]
where the time goes in v1:
time: 522 us; the launch traced here: 519 us
  blocking collectives  229 us (44%)
  local copies, waits for them, and re-layouts  116 us (22%)
  other arithmetic  67.9 us (13%)
  waiting for transfers between devices  60.5 us (12%)
  matrix products  30.5 us (6%)
  starting transfers between devices  14.8 us (3%)
    all_to_all x1, blocking collectives, local(): lax.all_to_all(weighted, 'mode', split_axis=2, concat_axis=0, tiled=True)  76.9 us
    all_to_all x1, blocking collectives, local(): lax.all_to_all(jnp.stack(jnp.split(modes_field, lax.axis_size('mode'), ax...  76.5 us
    all_to_all x1, blocking collectives, local(): lax.all_to_all(tendency, 'mode', split_axis=0, concat_axis=2, tiled=True)  75.2 us
    convert_element_type x1, other arithmetic, node_terms(): return (node_weights[:, None, None] * flux).astype(jnp.bfloat16)  60.8 us
    all_to_all x1, waiting for transfers between devices, local(): lax.all_to_all(nodal, 'mode', split_axis=0, concat_axis=2, tiled=True)  60.5 us
    unnamed x20, local copies, waits for them, and re-layouts  41.2 us
    all_to_all x2, local copies, waits for them, and re-layouts, local(): lax.all_to_all(nodal, 'mode', split_axis=0, concat_axis=2, tiled=True)  19.8 us
    dot_general x1, matrix products, node_terms(): jnp.einsum('qk,krc->qrc', node_points, kl_piece, precision=lax.Precision....  16.3 us
  transfers between devices with their start and end apart: 5, of which 1 were waited for; matrix products, arithmetic and copies ran while one was open for 6% of the time, Pallas kernels for 0%

profile of v1, /device:TPU:0, one launch (start us, length us, event | category | flops | bytes accessed | tf_op | source)
XLA Modules:
  0.0 518.9 jit_solution(8017692092937050127)
XLA Ops:
  0.0 0.0 copy-start
  0.0 1.2 bitcast_dynamic-update-slice_fusion.7
  1.2 1.2 bitcast_dynamic-update-slice_fusion.6
  2.5 1.2 bitcast_dynamic-update-slice_fusion.5
  3.7 1.2 bitcast_dynamic-update-slice_fusion.4
  5.0 1.2 bitcast_dynamic-update-slice_fusion.3
  6.2 1.2 bitcast_dynamic-update-slice_fusion.2
  7.5 1.2 bitcast_dynamic-update-slice_fusion.1
  8.7 1.2 bitcast_dynamic-update-slice_fusion
  9.9 76.5 %all_to_all.59 = bf16[8,64,48,128]{3,2,1,0:T(8,128)(2,1)S(1)} all-to-all(bf16[8,64,48,128]{3,2,1,0:T(8,128)(2,1)S(1)} %bitcast_dynamic-update-slice_fusion), channel_id=1, replica_groups=mesh['grid'=4,'mode'=8] {'mode'}, dimensions={0} | all-to-all | bytes 12582912 | tf_op jit(solution)/shard_map/all_to_all | solution.py:57
  86.4 0.0 copy-done
  86.5 6.0 %convert_bitcast_fusion.1 = bf16[512,48,128]{0,2,1:T(8,128)(2,1)} fusion(bf16[512,48,128]{2,1,0:T(8,128)(2,1)S(1)} %bitcast.62, bf16[512,512]{1,0:T(8,128)(2,1)S(1)} %copy-done), kind=kOutput, calls=%fused_computation.32 | convolution fusion | flops 3224371200 | bytes 13107200 | tf_op jit(solution)/shard_map/qp,prc->qrc/dot_general | solution.py:53
  92.5 9.1 %copy.47 = bf16[512,48,128]{2,1,0:T(8,128)(2,1)} copy(bf16[512,48,128]{0,2,1:T(8,128)(2,1)} %convert_bitcast_fusion.1) | data formatting | bytes 12582912 | tf_op jit(solution)/shard_map/convert_element_type | solution.py:64
  101.6 4.8 all-to-all-start.1
  106.3 0.0 copy-start.2
  106.4 3.8 copy.43
  110.1 0.0 copy-start.1
  110.1 1.7 copy-done.1
  111.8 3.5 collective-permute-start
  115.3 1.3 collective-permute-start.1
  116.6 0.8 dynamic_slice.6
  117.4 0.0 copy-done.2
  117.4 60.5 %all-to-all-done.1 = bf16[512,48,128]{2,1,0:T(8,128)(2,1)} async-done(((bf16[512,48,128]{2,1,0:T(8,128)(2,1)}), bf16[512,48,128]{2,1,0:T(8,128)(2,1)}, u32[]{:S(2)}, u32[]{:S(2)}) %all-to-all-start.1) | async-done | bytes 6291488 | tf_op jit(solution)/shard_map/all_to_all | solution.py:65
  177.9 9.5 %copy.48 = bf16[64,48,8,128]{3,2,0,1:T(8,128)(2,1)} copy(bf16[64,48,8,128]{3,1,0,2:T(8,128)(2,1)} %bitcast.13) | data formatting | bytes 12582912 | tf_op jit(solution)/shard_map/all_to_all | solution.py:65
  187.5 10.3 %all_to_all.46 = bf16[64,48,1024]{2,0,1:T(8,128)(2,1)} reshape(bf16[64,48,8,128]{3,2,0,1:T(8,128)(2,1)} %copy.48) | data formatting | bytes 12582912 | tf_op jit(solution)/shard_map/all_to_all | solution.py:65
  197.8 1.0 fusion.43
  198.8 3.5 collective-permute-start.2
  202.3 0.0 slice-start
  202.3 0.0 slice-start.1
  202.3 1.7 collective-permute-start.3
  204.0 0.0 collective-permute-done
  204.0 0.0 collective-permute-done.1
  204.0 16.3 %convolution_exponential_fusion = f32[64,50,1026]{2,0,1:T(8,128)} fusion(f32[16,1,1024]{2,0,1:T(8,128)S(1)} %collective-permute-done.1, f32[16,48,1024]{2,0,1:T(8,128)} %copy-done.1, f32[16,1,1024]{2,0,1:T(8,128)S(1)} %collective-permute-done, f32[512,16]{0,1:T(8,128)} %param.9, s32[]{:T(128)S(6)} %select_n.4), kind=kOutput, calls=%fused_computation.2 | convolution fusion | flops 636940800 | bytes 16417796 | tf_op jit(solution)/shard_map/qk,krc->qrc/dot_general | solution.py:27
  220.3 0.0 collective-permute-done.2
  220.4 0.0 collective-permute-done.3
  220.4 0.0 slice-done
  220.4 0.0 slice-done.1
  220.4 7.0 %fusion.20 = f32[64,50,1026]{2,0,1:T(8,128)} fusion(bf16[64,1,1024]{2,0,1:T(8,128)(2,1)S(1)} %collective-permute-done.3, bf16[64,48,1024]{2,0,1:T(8,128)(2,1)S(1)} %bitcast.59, bf16[64,1,1024]{2,0,1:T(8,128)(2,1)S(1)} %collective-permute-done.2), kind=kLoop, calls=%fused_computation.27 | loop fusion | flops 39398400 | bytes 19686400 | tf_op jit(solution)/shard_map/convert_element_type | solution.py:25
  227.4 60.8 %fusion.6 = bf16[64,48,1024]{2,0,1:T(8,128)(2,1)} fusion(f32[64,50,1026]{2,0,1:T(8,128)} %convolution_exponential_fusion, f32[64,50,1026]{2,0,1:T(8,128)} %fusion.20, f32[48,1024]{1,0:T(8,128)S(1)} %get-tuple-element.10, f32[48,1024]{1,0:T(8,128)S(1)} %get-tuple-element.9, f32[64]{0:T(128)S(1)} %dynamic_slice.6), kind=kLoop, calls=%fused_computation.10 | loop fusion | flops 84934656 | bytes 132514048 | tf_op jit(solution)/shard_map/convert_element_type | solution.py:47
  288.2 15.7 %copy.49 = bf16[64,48,1024]{0,1,2:T(8,128)(2,1)} copy(bf16[64,48,1024]{2,0,1:T(8,128)(2,1)} %fusion.6) | data formatting | bytes 12582912 | tf_op jit(solution)/shard_map/convert_element_type | solution.py:47
  303.9 13.7 %reshape.7 = bf16[8,2,196608]{2,1,0:T(2,128)(2,1)} reshape(bf16[1024,48,64]{2,1,0:T(8,128)(2,1)} %bitcast.56) | data formatting | bytes 12582912
  317.7 76.9 %all_to_all.60 = bf16[8,2,196608]{2,1,0:T(2,128)(2,1)} all-to-all(bf16[8,2,196608]{2,1,0:T(2,128)(2,1)} %reshape.7), channel_id=1, replica_groups=mesh['grid'=4,'mode'=8] {'mode'}, dimensions={0} | all-to-all | bytes 12582912 | tf_op jit(solution)/shard_map/all_to_all | solution.py:73
  394.5 13.3 %reshape.8 = bf16[1024,48,64]{2,1,0:T(8,128)(2,1)} reshape(bf16[8,2,196608]{2,1,0:T(2,128)(2,1)} %all_to_all.60) | data formatting | bytes 12582912
  407.9 14.1 %copy.57 = bf16[8,64,48,128]{3,1,0,2:T(8,128)(2,1)} copy(bf16[8,64,48,128]{1,2,3,0:T(8,128)(2,1)} %bitcast.57) | data formatting | bytes 12582912 | tf_op jit(solution)/shard_map/all_to_all | solution.py:73
  422.0 8.2 %convert_bitcast_fusion = bf16[512,48,128]{0,2,1:T(8,128)(2,1)} fusion(bf16[512,48,128]{2,0,1:T(8,128)(2,1)} %bitcast.61, bf16[512,512]{1,0:T(8,128)(2,1)S(1)} %copy-done), kind=kOutput, calls=%fused_computation.31 | convolution fusion | flops 3224371200 | bytes 13107200 | tf_op jit(solution)/shard_map/qp,qrc->prc/dot_general | solution.py:74
  430.2 9.0 %copy.53 = bf16[512,48,128]{2,1,0:T(8,128)(2,1)} copy(bf16[512,48,128]{0,2,1:T(8,128)(2,1)} %convert_bitcast_fusion) | data formatting | bytes 12582912 | tf_op jit(solution)/shard_map/convert_element_type | solution.py:77
  439.2 75.2 %all_to_all.61 = bf16[512,48,128]{2,1,0:T(8,128)(2,1)S(1)} all-to-all(bf16[512,48,128]{2,1,0:T(8,128)(2,1)} %copy.53), channel_id=1, replica_groups=mesh['grid'=4,'mode'=8] {'mode'}, dimensions={0} | all-to-all | bytes 12582912 | tf_op jit(solution)/shard_map/all_to_all | solution.py:78
  514.4 4.5 copy.64
  (3 shorter events, 0.0 us)
Async XLA Ops:
  0.0 86.4 %copy-start = (bf16[512,512]{1,0:T(8,128)(2,1)S(1)}, bf16[512,512]{1,0:T(8,128)(2,1)}, u32[]{:S(2)}) copy-start(bf16[512,512]{1,0:T(8,128)(2,1)} %param.7) | copy-start | bytes 1572868
  101.6 76.4 %all-to-all-start.1 = ((bf16[512,48,128]{2,1,0:T(8,128)(2,1)}), bf16[512,48,128]{2,1,0:T(8,128)(2,1)}, u32[]{:S(2)}, u32[]{:S(2)}) async-start(bf16[512,48,128]{2,1,0:T(8,128)(2,1)} %copy.47), calls=%async_computation.1 | async-start | bytes 12582912 | tf_op jit(solution)/shard_map/all_to_all | solution.py:65
  106.3 11.1 %copy-start.2 = (f32[2,48,1024]{2,1,0:T(8,128)S(1)}, f32[2,48,1024]{2,1,0:T(8,128)}, u32[]{:S(2)}) copy-start(f32[2,48,1024]{2,1,0:T(8,128)} %param.11) | copy-start | bytes 1179652
  110.1 1.7 copy-start.1
  111.8 92.2 %collective-permute-start = (f32[16,1,1024]{2,0,1:T(8,128)S(1)}, f32[16,1,1024]{2,0,1:T(8,128)S(1)}, u32[]{:S(2)}, u32[]{:S(2)}) collective-permute-start(f32[16,1,1024]{2,0,1:T(8,128)S(1)} %get-tuple-element.7), channel_id=1, source_target_pairs={{0,8},{8,16},{16,24},{1,9},{9,17},{17,25},{2,10},{10,18},{18,26},{... | collective-permute-start | bytes 196616 | tf_op jit(solution)/shard_map/ppermute | solution.py:15
  115.3 88.7 %collective-permute-start.1 = (f32[16,1,1024]{2,0,1:T(8,128)S(1)}, f32[16,1,1024]{2,0,1:T(8,128)S(1)}, u32[]{:S(2)}, u32[]{:S(2)}) collective-permute-start(f32[16,1,1024]{2,0,1:T(8,128)S(1)} %get-tuple-element.8), channel_id=1, source_target_pairs={{8,0},{16,8},{24,16},{9,1},{17,9},{25,17},{10,2},{18,10},{26,18},{... | collective-permute-start | bytes 196616 | tf_op jit(solution)/shard_map/ppermute | solution.py:17
  198.8 21.6 %collective-permute-start.2 = (bf16[64,1,1024]{2,0,1:T(8,128)(2,1)S(1)}, bf16[64,1,1024]{2,0,1:T(8,128)(2,1)S(1)}, u32[]{:S(2)}, u32[]{:S(2)}) collective-permute-start(bf16[64,1,1024]{2,0,1:T(8,128)(2,1)S(1)} %get-tuple-element.5), channel_id=1, source_target_pairs={{0,8},{8,16},{16,24},{1,9},{9,17},{17,25},{2,10},{10,18},{18,26},{... | collective-permute-start | bytes 393224 | tf_op jit(solution)/shard_map/ppermute | solution.py:15
  202.3 18.1 %slice-start = ((s8[6291456]{0:T(1024)(128)(4,1)}), s8[4194304]{0:T(1024)(128)(4,1)S(1)}, s32[]{:S(2)}) async-start(s8[6291456]{0:T(1024)(128)(4,1)} %bitcast.58), calls=%async_computation.4 | async-start | bytes 8388608
  202.3 18.1 %slice-start.1 = ((s8[6291456]{0:T(1024)(128)(4,1)}), s8[2097152]{0:T(1024)(128)(4,1)S(1)}, s32[]{:S(2)}) async-start(s8[6291456]{0:T(1024)(128)(4,1)} %bitcast.58), calls=%async_computation.5 | async-start | bytes 4194304
  202.3 18.1 %collective-permute-start.3 = (bf16[64,1,1024]{2,0,1:T(8,128)(2,1)S(1)}, bf16[64,1,1024]{2,0,1:T(8,128)(2,1)S(1)}, u32[]{:S(2)}, u32[]{:S(2)}) collective-permute-start(bf16[64,1,1024]{2,0,1:T(8,128)(2,1)S(1)} %get-tuple-element.6), channel_id=1, source_target_pairs={{8,0},{16,8},{24,16},{9,1},{17,9},{25,17},{10,2},{18,10},{26,18},{... | collective-permute-start | bytes 393224 | tf_op jit(solution)/shard_map/ppermute | solution.py:17
